TPU v7x, 32 devices: a whole 2x2x4 slice. The times are simulated.
32 devices in a mesh: expert: 16 (over z, y, core), dp: 2 (over x).
Axes of the slice: x: 2, y: 2, z: 4, core: 2. Of those that a mesh axis runs over, the one named last changes fastest.
Arguments:
- tokens: bfloat16 [4096, 2048], P(('expert', 'dp')), may hold values from -6 to 6
- cotangent: bfloat16 [4096, 2048], P(('expert', 'dp')), may hold values from -6 to 6
- expert_ids: int32 [4096, 6], P(('expert', 'dp')), may hold values from 0 to 15, all different within a row; in each aligned block of 128 rows (0 to 127, 128 to 255, ...) at most 60 rows name the same one
- gate_vals: float32 [4096, 6], P(('expert', 'dp')), may hold values from 0.05 to 0.5
- capacity: int32 [16], replicated, may hold values from 384 to 960
- w_gate: bfloat16 [16, 384, 2048], P('expert', 'dp'), may hold values from -0.125 to 0.125
- w_up: bfloat16 [16, 384, 2048], P('expert', 'dp'), may hold values from -0.125 to 0.125
- w_down: bfloat16 [16, 384, 2048], P('expert', 'dp'), may hold values from -0.3125 to 0.3125
Outputs:
- layer_out: bfloat16 [4096, 2048], P(('expert', 'dp'))
- grad_tokens: bfloat16 [4096, 2048], P(('expert', 'dp'))
- grad_gates: float32 [4096, 6], P(('expert', 'dp'))
- grad_gate_w: bfloat16 [16, 384, 2048], P('expert', 'dp')
- grad_up_w: bfloat16 [16, 384, 2048], P('expert', 'dp')
- grad_down_w: bfloat16 [16, 384, 2048], P('expert', 'dp')
Inputs may be any that keep to these rules, and one draw needn't show every extreme that they name: `expert_ids`: within the 128 rows of one device no expert is named more than 60 times, a bound that some block reaches.
All inputs are finite; a program needn't handle non-finite values.
Results may differ from a plain program's by a relative error of at most 0.0065.
Values may be sent and summed in bfloat16 or wider, within the bound.
No kernel may reach another device: no remote copies, remote signals or barrier semaphores. Data moves between devices by JAX's collectives and lax.ppermute only.
A program may use at most 128 MiB of HBM per device.

v0:
```python
import jax
import jax.numpy as jnp
from jax import lax
from jax.sharding import PartitionSpec as P


def entering(value, axis, join, neutral):
    count, mine = (lax.axis_size(axis), lax.axis_index(axis))
    pieces = lax.all_gather(value, axis)
    subtotal = jnp.full_like(value, 0) + jnp.asarray(neutral, value.dtype)

    def lap(position, subtotal):
        longer = join(subtotal, pieces[position])
        return jnp.where(position < mine, longer, subtotal)

    return lax.fori_loop(0, count - 1, lap, subtotal)


def add_counts(earlier, later):
    return earlier + later


def on_device(tokens, cotangent, expert_ids, gate_vals, capacity, w_gate, w_up, w_down):
    tok_rows, width = tokens.shape
    top_count = expert_ids.shape[1]
    experts = capacity.shape[0]
    local_experts = w_gate.shape[0]
    slots = max(2, (5 * tok_rows * top_count + 4 * experts - 1) // (4 * experts))
    n_expert = lax.axis_size("expert")
    flat_ids = expert_ids.reshape(-1)
    one_hot = (flat_ids[:, None] == jnp.arange(experts, dtype=jnp.int32)[None, :]).astype(jnp.int32)
    running = jnp.cumsum(one_hot, axis=0)
    local_rank = jnp.sum(running * one_hot, axis=1) - 1
    counts = running[-1]
    earlier = entering(counts, "expert", add_counts, jnp.zeros_like(counts))
    offset = jnp.sum(one_hot * earlier[None, :], axis=1)
    limit = jnp.sum(one_hot * capacity[None, :], axis=1)
    kept = offset + local_rank < limit
    slot_index = jnp.where(kept, flat_ids * slots + local_rank, experts * slots)
    input_routes = jnp.broadcast_to(tokens[:, None, :], (tok_rows, top_count, width)).reshape(
        -1, width
    )
    cot_routes = (
        (gate_vals[:, :, None] * cotangent.astype(jnp.float32)[:, None, :])
        .astype(jnp.bfloat16)
        .reshape(-1, width)
    )
    input_buf = (
        jnp.zeros((experts * slots, width), jnp.bfloat16)
        .at[slot_index]
        .set(input_routes, mode="drop")
    )
    cot_buf = (
        jnp.zeros((experts * slots, width), jnp.bfloat16)
        .at[slot_index]
        .set(cot_routes, mode="drop")
    )
    input_buf = input_buf.reshape(experts, slots, width)
    cot_buf = cot_buf.reshape(experts, slots, width)
    full_gate, full_up, full_down = (
        lax.all_gather(w_gate, "dp", axis=1, tiled=True),
        lax.all_gather(w_up, "dp", axis=1, tiled=True),
        lax.all_gather(w_down, "dp", axis=1, tiled=True),
    )
    rows_in, rows_cot = (
        lax.all_to_all(input_buf, "expert", split_axis=0, concat_axis=0, tiled=True),
        lax.all_to_all(cot_buf, "expert", split_axis=0, concat_axis=0, tiled=True),
    )
    rows_in = rows_in.reshape(n_expert, local_experts, slots, width)
    gate_pre = jnp.einsum("secd,efd->secf", rows_in, full_gate, preferred_element_type=jnp.float32)
    up_pre = jnp.einsum("secd,efd->secf", rows_in, full_up, preferred_element_type=jnp.float32)
    sigmoid_gate = jax.nn.sigmoid(gate_pre)
    activated = gate_pre * sigmoid_gate
    hidden = (activated * up_pre).astype(jnp.bfloat16)
    out_rows = jnp.einsum(
        "secf,efd->secd", hidden, full_down, preferred_element_type=jnp.float32
    ).astype(jnp.bfloat16)
    rows_cot = rows_cot.reshape(n_expert, local_experts, slots, width)
    d_hidden = jnp.einsum("secd,efd->secf", rows_cot, full_down, preferred_element_type=jnp.float32)
    d_gate = (d_hidden * up_pre * (sigmoid_gate + activated * (1.0 - sigmoid_gate))).astype(
        jnp.bfloat16
    )
    d_up = (d_hidden * activated).astype(jnp.bfloat16)
    dx_rows = jnp.einsum("secf,efd->secd", d_gate, full_gate, preferred_element_type=jnp.float32)
    dx_rows = (
        dx_rows + jnp.einsum("secf,efd->secd", d_up, full_up, preferred_element_type=jnp.float32)
    ).astype(jnp.bfloat16)
    part_down = jnp.einsum("secf,secd->efd", hidden, rows_cot, preferred_element_type=jnp.float32)
    part_gate = jnp.einsum("secf,secd->efd", d_gate, rows_in, preferred_element_type=jnp.float32)
    part_up = jnp.einsum("secf,secd->efd", d_up, rows_in, preferred_element_type=jnp.float32)
    summed_gate, summed_up, summed_down = (
        lax.psum_scatter(part_gate, "dp", scatter_dimension=1, tiled=True),
        lax.psum_scatter(part_up, "dp", scatter_dimension=1, tiled=True),
        lax.psum_scatter(part_down, "dp", scatter_dimension=1, tiled=True),
    )
    grad_gate_w = summed_gate.astype(jnp.bfloat16)
    grad_up_w = summed_up.astype(jnp.bfloat16)
    grad_down_w = summed_down.astype(jnp.bfloat16)
    out_rows = out_rows.reshape(n_expert * local_experts, slots, width)
    dx_rows = dx_rows.reshape(n_expert * local_experts, slots, width)
    back_out, back_dx = (
        lax.all_to_all(out_rows, "expert", split_axis=0, concat_axis=0, tiled=True),
        lax.all_to_all(dx_rows, "expert", split_axis=0, concat_axis=0, tiled=True),
    )
    picked_out = jnp.take(
        back_out.reshape(-1, width), slot_index, axis=0, mode="fill", fill_value=0
    )
    picked_dx = jnp.take(back_dx.reshape(-1, width), slot_index, axis=0, mode="fill", fill_value=0)
    picked_out = picked_out.reshape(tok_rows, top_count, width).astype(jnp.float32)
    picked_dx = picked_dx.reshape(tok_rows, top_count, width).astype(jnp.float32)
    layer_out = jnp.sum(gate_vals[:, :, None] * picked_out, axis=1).astype(jnp.bfloat16)
    grad_tokens = jnp.sum(picked_dx, axis=1).astype(jnp.bfloat16)
    grad_gates = jnp.sum(cotangent.astype(jnp.float32)[:, None, :] * picked_out, axis=-1)
    return (layer_out, grad_tokens, grad_gates, grad_gate_w, grad_up_w, grad_down_w)


def solution(mesh):
    placed = (
        P(("expert", "dp"), None),
        P(("expert", "dp"), None),
        P(("expert", "dp"), None),
        P(("expert", "dp"), None),
        P(),
        P("expert", "dp", None),
        P("expert", "dp", None),
        P("expert", "dp", None),
    )
    return jax.shard_map(
        on_device,
        mesh=mesh,
        in_specs=placed,
        out_specs=(
            P(("expert", "dp"), None),
            P(("expert", "dp"), None),
            P(("expert", "dp"), None),
            P("expert", "dp", None),
            P("expert", "dp", None),
            P("expert", "dp", None),
        ),
        check_vma=False,
    )
```

profile of v0, /device:TPU:13, one launch (start us, length us, event | category | flops | bytes accessed | tf_op | source)
XLA Modules:
  0.0 527.0 jit_solution(4731755545639999676)
XLA Ops:
  11.5 15.5 %all-gather = s32[16,1,16]{2,1,0:T(1,128)S(1)} all-gather(s32[1,1,16]{2,1,0:T(1,128)S(1)} %bitcast.121), channel_id=1, replica_groups=mesh['expert'=16,'dp'=2] {'expert'}, dimensions={0}, use_global_device_ids=true | all-gather | bytes 1088 | tf_op jit(solution)/shard_map/all_gather | solution.py:9
  32.0 4.9 reshape.202
  36.9 9.2 %scatter_custom_fusion = bf16[960,2048]{1,0:T(8,128)(2,1)} fusion(s32[768]{0:T(1024)S(1)} %fusion.27, bf16[768,2048]{1,0:T(8,128)(2,1)S(1)} %reshape.202, bf16[]{:T(256)} %constant.54.clone.1), kind=kCustom, calls=%fused_computation.19 | custom fusion | bytes 3932162 | tf_op jit(solution)/shard_map/scatter | solution.py:51
  46.1 4.9 reshape.170
  51.0 11.9 %all-to-all-start = ((bf16[16,60,2048]{2,1,0:T(8,128)(2,1)}), bf16[16,60,2048]{2,1,0:T(8,128)(2,1)}, u32[]{:S(2)}, u32[]{:S(2)}) async-start(bf16[16,60,2048]{2,1,0:T(8,128)(2,1)} %reshape.170), calls=%async_computation | async-start | bytes 8388608 | tf_op jit(solution)/shard_map/all_to_all | solution.py:66
  67.5 8.3 %mul.107 = f32[768,2048]{1,0:T(8,128)} reshape(f32[128,6,2048]{2,1,0:T(8,128)} %mul.106) | data formatting | bytes 12582912 | tf_op jit(solution)/shard_map/mul | solution.py:44
  75.7 14.3 %scatter_custom_fusion.1 = bf16[960,2048]{1,0:T(8,128)(2,1)} fusion(s32[768]{0:T(1024)S(1)} %fusion.27, f32[768,2048]{1,0:T(8,128)} %mul.107, f32[768]{0:T(1024)S(1)} %mul.104, bf16[]{:T(256)} %constant.54.clone.1), kind=kCustom, calls=%fused_computation.11 | custom fusion | flops 3145728 | bytes 10227714 | tf_op jit(solution)/shard_map/scatter | solution.py:56
  90.1 4.9 reshape.176
  94.9 60.3 %all-to-all-done = bf16[16,60,2048]{2,1,0:T(8,128)(2,1)} async-done(((bf16[16,60,2048]{2,1,0:T(8,128)(2,1)}), bf16[16,60,2048]{2,1,0:T(8,128)(2,1)}, u32[]{:S(2)}, u32[]{:S(2)}) %all-to-all-start) | async-done | bytes 3932192 | tf_op jit(solution)/shard_map/all_to_all | solution.py:66
  162.6 27.8 %all-gather.7.cloned.1.call-done = bf16[1,384,2048]{2,1,0:T(8,128)(2,1)} async-done(((bf16[1,192,2048]{2,1,0:T(8,128)(2,1)}), bf16[1,384,2048]{2,1,0:T(8,128)(2,1)}) %all-gather.7.cloned.1.call-update) | async-done | bytes 1572880 | tf_op jit(solution)/shard_map/all_gather | solution.py:62
  190.3 6.2 %fusion.13 = f32[16,60,384]{2,1,0:T(8,128)} fusion(bf16[16,60,2048]{2,1,0:T(8,128)(2,1)} %all-to-all-done, bf16[1,384,2048]{2,1,0:T(8,128)(2,1)} %all-gather.7.cloned.1.call-done), kind=kOutput, calls=%fused_computation.32 | convolution fusion | flops 1509949440 | bytes 6979584 | tf_op jit(solution)/shard_map/secd,efd->secf/dot_general | solution.py:71
  196.5 22.6 %all-gather.9.cloned.1.call-done = bf16[1,384,2048]{2,1,0:T(8,128)(2,1)} async-done(((bf16[1,192,2048]{2,1,0:T(8,128)(2,1)}), bf16[1,384,2048]{2,1,0:T(8,128)(2,1)}) %all-gather.9.cloned.1.call-update) | async-done | bytes 1572880 | tf_op jit(solution)/shard_map/all_gather | solution.py:63
  219.1 33.5 %all-to-all-done.2 = bf16[16,60,2048]{2,1,0:T(8,128)(2,1)} async-done(((bf16[16,60,2048]{2,1,0:T(8,128)(2,1)}), bf16[16,60,2048]{2,1,0:T(8,128)(2,1)}, u32[]{:S(2)}, u32[]{:S(2)}) %all-to-all-start.2) | async-done | bytes 3932192 | tf_op jit(solution)/shard_map/all_to_all | solution.py:67
  252.6 6.2 %fusion.9 = f32[16,60,384]{2,1,0:T(8,128)} fusion(bf16[16,60,2048]{2,1,0:T(8,128)(2,1)} %all-to-all-done.2, bf16[1,384,2048]{2,1,0:T(8,128)(2,1)} %all-gather.9.cloned.1.call-done), kind=kOutput, calls=%fused_computation.28 | convolution fusion | flops 1509949440 | bytes 6979584 | tf_op jit(solution)/shard_map/secd,efd->secf/dot_general | solution.py:79
  258.8 6.4 %fusion.23 = (bf16[16,60,384]{2,1,0:T(8,128)(2,1)S(1)}, bf16[16,1,60,384]{3,2,0,1:T(8,128)(2,1)S(1)}, bf16[16,60,384]{2,1,0:T(8,128)(2,1)S(1)}) fusion(f32[16,60,384]{2,1,0:T(8,128)} %fusion.9, f32[16,60,384]{2,1,0:T(8,128)} %fusion.13, bf16[16,60,2048]{2,1,0:T(8,128)(2,1)} %all-to-all-done, bf16[1,384,2048]{2,1,0:T(8,128)(2,1)} %all-gather.5.cloned.1.call-done), kind=kOutput, calls=%fused_computation.44 | convolution fusion | flops 1515110400 | bytes 10665984 | tf_op jit(solution)/shard_map/secd,efd->secf/dot_general | solution.py:70
  265.2 5.7 %convolution_bitcast_fusion = f32[1,384,2048]{2,1,0:T(8,128)} fusion(bf16[16,60,384]{2,1,0:T(8,128)(2,1)S(1)} %get-tuple-element.135, bf16[16,60,2048]{2,1,0:T(8,128)(2,1)} %all-to-all-done.2), kind=kOutput, calls=%fused_computation.15 | convolution fusion | flops 1509949440 | bytes 7815168 | tf_op jit(solution)/shard_map/secf,secd->efd/dot_general | solution.py:88
  270.9 5.7 %convolution_convert_fusion = bf16[16,60,2048]{2,1,0:T(8,128)(2,1)} fusion(bf16[16,60,384]{2,1,0:T(8,128)(2,1)S(1)} %get-tuple-element.135, bf16[1,384,2048]{2,1,0:T(8,128)(2,1)} %all-gather.9.cloned.1.call-done), kind=kOutput, calls=%fused_computation.10 | convolution fusion | flops 1511915520 | bytes 6242304 | tf_op jit(solution)/shard_map/secf,efd->secd/dot_general | solution.py:75
  276.6 4.9 all-to-all-start.1
  281.8 5.6 %convolution_bitcast_fusion.2 = f32[1,384,2048]{2,1,0:T(8,128)} fusion(bf16[16,60,2048]{2,1,0:T(8,128)(2,1)} %all-to-all-done, bf16[16,1,60,384]{3,2,0,1:T(8,128)(2,1)S(1)} %get-tuple-element.134), kind=kOutput, calls=%fused_computation.17 | convolution fusion | flops 1509949440 | bytes 7815168 | tf_op jit(solution)/shard_map/secf,secd->efd/dot_general | solution.py:89
  295.7 78.3 %all-to-all-done.1 = bf16[16,60,2048]{2,1,0:T(8,128)(2,1)} async-done(((bf16[16,60,2048]{2,1,0:T(8,128)(2,1)}), bf16[16,60,2048]{2,1,0:T(8,128)(2,1)}, u32[]{:S(2)}, u32[]{:S(2)}) %all-to-all-start.1) | async-done | bytes 3932192 | tf_op jit(solution)/shard_map/all_to_all | solution.py:102
  374.0 4.9 all-to-all-start.3
  379.0 5.7 %convolution_bitcast_fusion.1 = f32[1,384,2048]{2,1,0:T(8,128)} fusion(bf16[16,60,384]{2,1,0:T(8,128)(2,1)S(1)} %get-tuple-element.133, bf16[16,60,2048]{2,1,0:T(8,128)(2,1)} %all-to-all-done), kind=kOutput, calls=%fused_computation.16 | convolution fusion | flops 1509949440 | bytes 7815168 | tf_op jit(solution)/shard_map/secf,secd->efd/dot_general | solution.py:90
  389.5 39.2 %reduce-scatter.6.cloned.1.call-done = f32[1,192,2048]{2,1,0:T(8,128)} async-done(((f32[1,384,2048]{2,1,0:T(8,128)}), f32[1,192,2048]{2,1,0:T(8,128)}) %reduce-scatter.6.cloned.1.call-update) | async-done | bytes 1572880 | tf_op jit(solution)/shard_map/reduce_scatter | solution.py:93
  431.1 5.1 reshape.175
  436.3 9.0 %gather_fusion = bf16[768,2048]{1,0:T(8,128)(2,1)S(1)} fusion(bf16[960,2048]{1,0:T(8,128)(2,1)} %reshape.175, s32[1024]{0:T(1024)S(1)} %pad_clamp_fusion), kind=kCustom, calls=%fused_computation.clone | custom fusion | bytes 6294528 | tf_op jit(solution)/shard_map/jit(_take)/gather | solution.py:105
  449.8 21.6 %all-to-all-done.3 = bf16[16,60,2048]{2,1,0:T(8,128)(2,1)} async-done(((bf16[16,60,2048]{2,1,0:T(8,128)(2,1)}), bf16[16,60,2048]{2,1,0:T(8,128)(2,1)}, u32[]{:S(2)}, u32[]{:S(2)}) %all-to-all-start.3) | async-done | bytes 3932192 | tf_op jit(solution)/shard_map/all_to_all | solution.py:103
  476.2 9.7 %gather_fusion.1 = bf16[768,2048]{1,0:T(8,128)(2,1)} fusion(bf16[960,2048]{1,0:T(8,128)(2,1)} %reshape.179, s32[1024]{0:T(1024)S(1)} %pad_clamp_fusion), kind=kCustom, calls=%fused_computation.1.clone | custom fusion | bytes 6294528 | tf_op jit(solution)/shard_map/jit(_take)/gather | solution.py:108
  486.0 6.2 %broadcast_select_fusion.2 = (bf16[768,2048]{1,0:T(8,128)(2,1)}, f32[768,2048]{1,0:T(8,128)}) fusion(bf16[768,2048]{1,0:T(8,128)(2,1)} %gather_fusion.1, pred[768]{0:T(1024)(128)(4,1)S(1)} %get-tuple-element.131, bf16[768,2048]{1,0:T(8,128)(2,1)S(1)} %gather_fusion), kind=kLoop, calls=%fused_computation.14 | loop fusion | flops 4718592 | bytes 15729408 | tf_op jit(solution)/shard_map/jit(_take)/select_n | solution.py:108
  492.2 6.3 %reshape.180 = bf16[128,6,2048]{2,1,0:T(8,128)(2,1)} reshape(bf16[768,2048]{1,0:T(8,128)(2,1)} %get-tuple-element.136) | data formatting | bytes 6291456 | tf_op jit(solution)/shard_map/reshape | solution.py:110
  498.5 5.7 %reduce_sum.69 = bf16[128,2048]{1,0:T(8,128)(2,1)} reduce(bf16[128,6,2048]{2,1,0:T(8,128)(2,1)} %reshape.180, bf16[]{:T(256)} %constant.54.clone.1), dimensions={1}, to_apply=%region_10.12 | reduce | flops 1310720 | bytes 3670018 | tf_op jit(solution)/shard_map/reduce_sum | solution.py:112
  504.1 8.1 %reshape.181 = f32[128,6,2048]{2,1,0:T(8,128)} reshape(f32[768,2048]{1,0:T(8,128)} %get-tuple-element.137) | data formatting | bytes 12582912 | tf_op jit(solution)/shard_map/convert_element_type | solution.py:109
  512.3 7.4 %multiply_reduce_fusion = bf16[128,2048]{1,0:T(8,128)(2,1)} fusion(f32[128,6,2048]{2,1,0:T(8,128)} %reshape.181, f32[128,6]{1,0:T(8,128)S(1)} %copy.29), kind=kLoop, calls=%fused_computation.7 | loop fusion | flops 2883584 | bytes 6818816 | tf_op jit(solution)/shard_map/reduce_sum | solution.py:111
  (71 shorter events, 46.5 us)
Async XLA Ops:
  51.0 11.9 %copy-start.3 = (f32[128,6]{0,1:T(8,128)S(1)}, f32[128,6]{0,1:T(8,128)}, u32[]{:S(2)}) copy-start(f32[128,6]{0,1:T(8,128)} %param.15) | copy-start | bytes 9220
  51.0 12.1 %copy-start.2 = (bf16[128,2048]{1,0:T(8,128)(2,1)S(1)}, bf16[128,2048]{1,0:T(8,128)(2,1)}, u32[]{:S(2)}) copy-start(bf16[128,2048]{1,0:T(8,128)(2,1)} %param.13) | copy-start | bytes 1572868
  51.0 104.2 %all-to-all-start = ((bf16[16,60,2048]{2,1,0:T(8,128)(2,1)}), bf16[16,60,2048]{2,1,0:T(8,128)(2,1)}, u32[]{:S(2)}, u32[]{:S(2)}) async-start(bf16[16,60,2048]{2,1,0:T(8,128)(2,1)} %reshape.170), calls=%async_computation | async-start | bytes 8388608 | tf_op jit(solution)/shard_map/all_to_all | solution.py:66
  155.3 97.3 %all-to-all-start.2 = ((bf16[16,60,2048]{2,1,0:T(8,128)(2,1)}), bf16[16,60,2048]{2,1,0:T(8,128)(2,1)}, u32[]{:S(2)}, u32[]{:S(2)}) async-start(bf16[16,60,2048]{2,1,0:T(8,128)(2,1)} %reshape.176), calls=%async_computation.2 | async-start | bytes 8388608 | tf_op jit(solution)/shard_map/all_to_all | solution.py:67
  160.1 30.2 %all-gather.7.cloned.1.call-start = ((), (), s32[]{:S(2)}) async-start(), calls=%async_computation.8 | async-start | bytes 2359296 | tf_op jit(solution)/shard_map/all_gather | solution.py:62
  160.8 58.2 %all-gather.9.cloned.1.call-start = ((), (), s32[]{:S(2)}) async-start(), calls=%async_computation.9 | async-start | bytes 2359296 | tf_op jit(solution)/shard_map/all_gather | solution.py:63
  161.6 97.2 %all-gather.5.cloned.1.call-start = ((), (), s32[]{:S(2)}) async-start(), calls=%async_computation.7 | async-start | bytes 2359296 | tf_op jit(solution)/shard_map/all_gather | solution.py:61
  162.3 222.4 %reduce-scatter.8.cloned.1.call-start = ((), (), s32[]{:S(2)}) async-start(), calls=%async_computation.12 | async-start | bytes 4718592 | tf_op jit(solution)/shard_map/reduce_scatter | solution.py:94
  276.6 97.4 %all-to-all-start.1 = ((bf16[16,60,2048]{2,1,0:T(8,128)(2,1)}), bf16[16,60,2048]{2,1,0:T(8,128)(2,1)}, u32[]{:S(2)}, u32[]{:S(2)}) async-start(bf16[16,60,2048]{2,1,0:T(8,128)(2,1)} %convolution_convert_fusion), calls=%async_computation.1 | async-start | bytes 8388608 | tf_op jit(solution)/shard_map/all_to_all | solution.py:102
  281.6 105.6 %reduce-scatter.4.cloned.1.call-start = ((), (), s32[]{:S(2)}) async-start(), calls=%async_computation.10 | async-start | bytes 4718592 | tf_op jit(solution)/shard_map/reduce_scatter | solution.py:92
  287.4 1.5 copy-start.1
  288.9 2.3 copy-start
  374.0 97.4 %all-to-all-start.3 = ((bf16[16,60,2048]{2,1,0:T(8,128)(2,1)}), bf16[16,60,2048]{2,1,0:T(8,128)(2,1)}, u32[]{:S(2)}, u32[]{:S(2)}) async-start(bf16[16,60,2048]{2,1,0:T(8,128)(2,1)} %add_convert_fusion), calls=%async_computation.3 | async-start | bytes 8388608 | tf_op jit(solution)/shard_map/all_to_all | solution.py:103
  378.9 49.8 %reduce-scatter.6.cloned.1.call-start = ((), (), s32[]{:S(2)}) async-start(), calls=%async_computation.11 | async-start | bytes 4718592 | tf_op jit(solution)/shard_map/reduce_scatter | solution.py:93
Sparse Core Ops, SparseCore 0:
  162.5 27.7 all-gather.6
  191.8 27.2 all-gather.8
  220.6 27.1 all-gather.4
  271.0 42.8 reduce-scatter.7
  316.1 43.3 reduce-scatter.3
  384.8 43.8 reduce-scatter.5
where the time goes:
time: 535 us; the launch traced here: 527 us
  waiting for transfers between devices  285 us (53%)
  local copies, waits for them, and re-layouts  87.3 us (16%)
  matrix products  48.3 us (9%)
  other arithmetic  48.1 us (9%)
  starting transfers between devices  27.2 us (5%)
  blocking collectives  15.5 us (3%)
  between operations  14.8 us (3%)
    all_to_all x1, waiting for transfers between devices, on_device(): lax.all_to_all(out_rows, 'expert', split_axis=0, concat_axis=0, tiled=True)  78.3 us
    all_to_all x1, waiting for transfers between devices, on_device(): lax.all_to_all(input_buf, 'expert', split_axis=0, concat_axis=0, tiled=True)  60.3 us
    reduce_scatter x1, waiting for transfers between devices, on_device(): lax.psum_scatter(part_up, 'dp', scatter_dimension=1, tiled=True)  39.2 us
    all_to_all x1, waiting for transfers between devices, on_device(): lax.all_to_all(cot_buf, 'expert', split_axis=0, concat_axis=0, tiled=True)  33.5 us
    all_gather x1, waiting for transfers between devices, on_device(): lax.all_gather(w_up, 'dp', axis=1, tiled=True)  27.8 us
    all_gather x1, waiting for transfers between devices, on_device(): lax.all_gather(w_down, 'dp', axis=1, tiled=True)  22.6 us
    all_to_all x1, waiting for transfers between devices, on_device(): lax.all_to_all(dx_rows, 'expert', split_axis=0, concat_axis=0, tiled=True)  21.6 us
    all_gather x1, blocking collectives, entering(): pieces = lax.all_gather(value, axis)  15.5 us
  transfers between devices with their start and end apart: 10, of which 7 were waited for; matrix products, arithmetic and copies ran while one was open for 18% of the time, Pallas kernels for 0%

commit v1 on v0

--- a/solution.py
+++ b/solution.py
@@ -2,6 +2,29 @@
 import jax.numpy as jnp
 from jax import lax
 from jax.sharding import PartitionSpec as P
+
+
+def split_up(x, dim, count):
+    before, after = (x.shape[:dim], x.shape[dim + 1 :])
+    return jnp.moveaxis(x.reshape(*before, count, -1, *after), dim, 0)
+
+
+def in_order(blocks, dim):
+    blocks = jnp.moveaxis(blocks, 0, dim)
+    shape = blocks.shape
+    return blocks.reshape(*shape[:dim], shape[dim] * shape[dim + 1], *shape[dim + 2 :])
+
+
+def sent_to_each(x, axis, split_dim, concat_dim):
+    peers, mine = (lax.axis_size(axis), lax.axis_index(axis))
+    pieces = split_up(x, split_dim, peers)
+    out = pieces
+    for step in range(1, peers):
+        target, source = ((mine + step) % peers, (mine - step) % peers)
+        sent = lax.dynamic_index_in_dim(pieces, target, 0)
+        received = lax.ppermute(sent, axis, [(i, (i + step) % peers) for i in range(peers)])
+        out = lax.dynamic_update_slice_in_dim(out, received, source, axis=0)
+    return in_order(out, concat_dim)
 
 
 def entering(value, axis, join, neutral):
@@ -100,7 +123,7 @@
     dx_rows = dx_rows.reshape(n_expert * local_experts, slots, width)
     back_out, back_dx = (
         lax.all_to_all(out_rows, "expert", split_axis=0, concat_axis=0, tiled=True),
-        lax.all_to_all(dx_rows, "expert", split_axis=0, concat_axis=0, tiled=True),
+        sent_to_each(dx_rows, "expert", 0, 0),
     )
     picked_out = jnp.take(
         back_out.reshape(-1, width), slot_index, axis=0, mode="fill", fill_value=0

time: 535 us -> 577 us (1.079)
  the two profiles are of different devices: /device:TPU:13 before, /device:TPU:29 now
where the time goes in v1:
time: 577 us; the launch traced here: 570 us
  waiting for transfers between devices  251 us (44%)
  local copies, waits for them, and re-layouts  103 us (18%)
  starting transfers between devices  88.9 us (15%)
  other arithmetic  48.1 us (8%)
  matrix products  46.5 us (8%)
  blocking collectives  16.8 us (3%)
  between operations  15.1 us (3%)
    ppermute x15, waiting for transfers between devices, sent_to_each(): lax.ppermute(sent, axis, [(i, (i + step) % peers) for i in range(peers)])  107 us
    ppermute x15, starting transfers between devices, sent_to_each(): lax.ppermute(sent, axis, [(i, (i + step) % peers) for i in range(peers)])  66.1 us
    all_to_all x1, waiting for transfers between devices, on_device(): lax.all_to_all(input_buf, 'expert', split_axis=0, concat_axis=0, tiled=True)  59.3 us
    all_to_all x1, waiting for transfers between devices, on_device(): lax.all_to_all(cot_buf, 'expert', split_axis=0, concat_axis=0, tiled=True)  32.5 us
    all_gather x1, waiting for transfers between devices, on_device(): lax.all_gather(w_up, 'dp', axis=1, tiled=True)  27.8 us
    all_gather x1, waiting for transfers between devices, on_device(): lax.all_gather(w_down, 'dp', axis=1, tiled=True)  22.6 us
    all_gather x1, blocking collectives, entering(): pieces = lax.all_gather(value, axis)  16.8 us
    scatter x1, other arithmetic, on_device(): cot_buf = jnp.zeros((experts * slots, width), jnp.bfloat16).at[slot_index...  14.3 us
  transfers between devices with their start and end apart: 24, of which 11 were waited for; matrix products, arithmetic and copies ran while one was open for 18% of the time, Pallas kernels for 0%

profile of v1, /device:TPU:29, one launch (start us, length us, event | category | flops | bytes accessed | tf_op | source)
XLA Modules:
  0.0 569.6 jit_solution(3207785282557548299)
XLA Ops:
  11.5 16.8 %all-gather = s32[16,1,16]{2,1,0:T(1,128)S(1)} all-gather(s32[1,1,16]{2,1,0:T(1,128)S(1)} %bitcast.219), channel_id=1, replica_groups=mesh['expert'=16,'dp'=2] {'expert'}, dimensions={0}, use_global_device_ids=true | all-gather | bytes 1088 | tf_op jit(solution)/shard_map/all_gather | solution.py:32
  38.2 9.2 %scatter_custom_fusion = bf16[960,2048]{1,0:T(8,128)(2,1)} fusion(s32[768]{0:T(1024)S(1)} %fusion.27, bf16[768,2048]{1,0:T(8,128)(2,1)S(1)} %reshape.257, bf16[]{:T(256)} %constant.242.clone.1), kind=kCustom, calls=%fused_computation.19 | custom fusion | bytes 3932162 | tf_op jit(solution)/shard_map/scatter | solution.py:74
  52.3 10.5 %all-to-all-start = ((bf16[16,60,2048]{2,1,0:T(8,128)(2,1)}), bf16[16,60,2048]{2,1,0:T(8,128)(2,1)}, u32[]{:S(2)}, u32[]{:S(2)}) async-start(bf16[16,60,2048]{2,1,0:T(8,128)(2,1)} %reshape.211), calls=%async_computation | async-start | bytes 8388608 | tf_op jit(solution)/shard_map/all_to_all | solution.py:89
  67.3 8.3 %mul.107 = f32[768,2048]{1,0:T(8,128)} reshape(f32[128,6,2048]{2,1,0:T(8,128)} %mul.106) | data formatting | bytes 12582912 | tf_op jit(solution)/shard_map/mul | solution.py:67
  75.6 14.3 %scatter_custom_fusion.1 = bf16[960,2048]{1,0:T(8,128)(2,1)} fusion(s32[768]{0:T(1024)S(1)} %fusion.27, f32[768,2048]{1,0:T(8,128)} %mul.107, f32[768]{0:T(1024)S(1)} %mul.104, bf16[]{:T(256)} %constant.242.clone.1), kind=kCustom, calls=%fused_computation.11 | custom fusion | flops 3145728 | bytes 10227714 | tf_op jit(solution)/shard_map/scatter | solution.py:79
  94.8 59.3 %all-to-all-done = bf16[16,60,2048]{2,1,0:T(8,128)(2,1)} async-done(((bf16[16,60,2048]{2,1,0:T(8,128)(2,1)}), bf16[16,60,2048]{2,1,0:T(8,128)(2,1)}, u32[]{:S(2)}, u32[]{:S(2)}) %all-to-all-start) | async-done | bytes 3932192 | tf_op jit(solution)/shard_map/all_to_all | solution.py:89
  154.0 5.9 %all-to-all-start.2 = ((bf16[16,60,2048]{2,1,0:T(8,128)(2,1)}), bf16[16,60,2048]{2,1,0:T(8,128)(2,1)}, u32[]{:S(2)}, u32[]{:S(2)}) async-start(bf16[16,60,2048]{2,1,0:T(8,128)(2,1)} %reshape.217), calls=%async_computation.2 | async-start | bytes 8388608 | tf_op jit(solution)/shard_map/all_to_all | solution.py:90
  162.3 27.8 %all-gather.7.cloned.1.call-done = bf16[1,384,2048]{2,1,0:T(8,128)(2,1)} async-done(((bf16[1,192,2048]{2,1,0:T(8,128)(2,1)}), bf16[1,384,2048]{2,1,0:T(8,128)(2,1)}) %all-gather.7.cloned.1.call-update) | async-done | bytes 1572880 | tf_op jit(solution)/shard_map/all_gather | solution.py:85
  190.1 6.2 %fusion.13 = f32[16,60,384]{2,1,0:T(8,128)} fusion(bf16[16,60,2048]{2,1,0:T(8,128)(2,1)} %all-to-all-done, bf16[1,384,2048]{2,1,0:T(8,128)(2,1)} %all-gather.7.cloned.1.call-done), kind=kOutput, calls=%fused_computation.32 | convolution fusion | flops 1509949440 | bytes 6979584 | tf_op jit(solution)/shard_map/secd,efd->secf/dot_general | solution.py:94
  196.4 22.6 %all-gather.9.cloned.1.call-done = bf16[1,384,2048]{2,1,0:T(8,128)(2,1)} async-done(((bf16[1,192,2048]{2,1,0:T(8,128)(2,1)}), bf16[1,384,2048]{2,1,0:T(8,128)(2,1)}) %all-gather.9.cloned.1.call-update) | async-done | bytes 1572880 | tf_op jit(solution)/shard_map/all_gather | solution.py:86
  218.9 32.5 %all-to-all-done.2 = bf16[16,60,2048]{2,1,0:T(8,128)(2,1)} async-done(((bf16[16,60,2048]{2,1,0:T(8,128)(2,1)}), bf16[16,60,2048]{2,1,0:T(8,128)(2,1)}, u32[]{:S(2)}, u32[]{:S(2)}) %all-to-all-start.2) | async-done | bytes 3932192 | tf_op jit(solution)/shard_map/all_to_all | solution.py:90
  251.4 6.2 %fusion.9 = f32[16,60,384]{2,1,0:T(8,128)} fusion(bf16[16,60,2048]{2,1,0:T(8,128)(2,1)} %all-to-all-done.2, bf16[1,384,2048]{2,1,0:T(8,128)(2,1)} %all-gather.9.cloned.1.call-done), kind=kOutput, calls=%fused_computation.28 | convolution fusion | flops 1509949440 | bytes 6979584 | tf_op jit(solution)/shard_map/secd,efd->secf/dot_general | solution.py:102
  257.6 6.4 %fusion.23 = (bf16[16,60,384]{2,1,0:T(8,128)(2,1)S(1)}, bf16[16,1,60,384]{3,2,0,1:T(8,128)(2,1)S(1)}, bf16[16,60,384]{2,1,0:T(8,128)(2,1)S(1)}) fusion(f32[16,60,384]{2,1,0:T(8,128)} %fusion.9, f32[16,60,384]{2,1,0:T(8,128)} %fusion.13, bf16[16,60,2048]{2,1,0:T(8,128)(2,1)} %all-to-all-done, bf16[1,384,2048]{2,1,0:T(8,128)(2,1)} %all-gather.5.cloned.1.call-done), kind=kOutput, calls=%fused_computation.44 | convolution fusion | flops 1515110400 | bytes 10665984 | tf_op jit(solution)/shard_map/secd,efd->secf/dot_general | solution.py:93
  264.1 5.7 %convolution_bitcast_fusion = f32[1,384,2048]{2,1,0:T(8,128)} fusion(bf16[16,60,384]{2,1,0:T(8,128)(2,1)S(1)} %get-tuple-element.150, bf16[16,60,2048]{2,1,0:T(8,128)(2,1)} %all-to-all-done.2), kind=kOutput, calls=%fused_computation.15 | convolution fusion | flops 1509949440 | bytes 7815168 | tf_op jit(solution)/shard_map/secf,secd->efd/dot_general | solution.py:111
  269.8 5.6 convolution_bitcast_fusion.2
  275.5 5.7 %convolution_convert_fusion = bf16[16,60,2048]{2,1,0:T(8,128)(2,1)} fusion(bf16[16,60,384]{2,1,0:T(8,128)(2,1)S(1)} %get-tuple-element.150, bf16[1,384,2048]{2,1,0:T(8,128)(2,1)} %all-gather.9.cloned.1.call-done), kind=kOutput, calls=%fused_computation.10 | convolution fusion | flops 1511915520 | bytes 6242304 | tf_op jit(solution)/shard_map/secf,efd->secd/dot_general | solution.py:98
  281.2 5.9 %all-to-all-start.1 = ((bf16[16,60,2048]{2,1,0:T(8,128)(2,1)}), bf16[16,60,2048]{2,1,0:T(8,128)(2,1)}, u32[]{:S(2)}, u32[]{:S(2)}) async-start(bf16[16,60,2048]{2,1,0:T(8,128)(2,1)} %convolution_convert_fusion), calls=%async_computation.1 | async-start | bytes 8388608 | tf_op jit(solution)/shard_map/all_to_all | solution.py:125
  287.3 5.8 %convolution_bitcast_fusion.1 = f32[1,384,2048]{2,1,0:T(8,128)} fusion(bf16[16,60,384]{2,1,0:T(8,128)(2,1)S(1)} %get-tuple-element.148, bf16[16,60,2048]{2,1,0:T(8,128)(2,1)} %all-to-all-done), kind=kOutput, calls=%fused_computation.16 | convolution fusion | flops 1509949440 | bytes 7815168 | tf_op jit(solution)/shard_map/secf,secd->efd/dot_general | solution.py:113
  307.3 53.5 %collective-permute-done = bf16[1,1,60,2048]{3,2,0,1:T(8,128)(2,1)} collective-permute-done((bf16[1,1,60,2048]{3,2,0,1:T(8,128)(2,1)}, bf16[1,1,60,2048]{3,2,0,1:T(8,128)(2,1)}, u32[]{:S(2)}, u32[]{:S(2)}) %collective-permute-start) | collective-permute-done | bytes 245792 | tf_op jit(solution)/shard_map/ppermute | solution.py:25
  371.9 25.2 %collective-permute-start.4 = (bf16[1,1,60,2048]{3,2,0,1:T(8,128)(2,1)S(1)}, bf16[1,1,60,2048]{3,2,0,1:T(8,128)(2,1)S(1)}, u32[]{:S(2)}, u32[]{:S(2)}) collective-permute-start(bf16[1,1,60,2048]{3,2,0,1:T(8,128)(2,1)S(1)} %get-tuple-element.143), channel_id=1, source_target_pairs={{0,10},{2,12},{4,14},{6,16},{8,18},{10,20},{12,22},{14,24},{16,26}... | collective-permute-start | bytes 737288 | tf_op jit(solution)/shard_map/ppermute | solution.py:25
  403.7 14.2 %collective-permute-start.6 = (bf16[1,1,60,2048]{3,2,0,1:T(8,128)(2,1)S(1)}, bf16[1,1,60,2048]{3,2,0,1:T(8,128)(2,1)S(1)}, u32[]{:S(2)}, u32[]{:S(2)}) collective-permute-start(bf16[1,1,60,2048]{3,2,0,1:T(8,128)(2,1)S(1)} %get-tuple-element.141), channel_id=1, source_target_pairs={{0,14},{2,16},{4,18},{6,20},{8,22},{10,24},{12,26},{14,28},{16,30}... | collective-permute-start | bytes 737288 | tf_op jit(solution)/shard_map/ppermute | solution.py:25
  418.7 9.4 %collective-permute-start.7 = (bf16[1,1,60,2048]{3,2,0,1:T(8,128)(2,1)S(1)}, bf16[1,1,60,2048]{3,2,0,1:T(8,128)(2,1)S(1)}, u32[]{:S(2)}, u32[]{:S(2)}) collective-permute-start(bf16[1,1,60,2048]{3,2,0,1:T(8,128)(2,1)S(1)} %get-tuple-element.140), channel_id=1, source_target_pairs={{0,16},{2,18},{4,20},{6,22},{8,24},{10,26},{12,28},{14,30},{16,0},... | collective-permute-start | bytes 737288 | tf_op jit(solution)/shard_map/ppermute | solution.py:25
  435.2 15.9 %collective-permute-done.7 = bf16[1,1,60,2048]{3,2,0,1:T(8,128)(2,1)S(1)} collective-permute-done((bf16[1,1,60,2048]{3,2,0,1:T(8,128)(2,1)S(1)}, bf16[1,1,60,2048]{3,2,0,1:T(8,128)(2,1)S(1)}, u32[]{:S(2)}, u32[]{:S(2)}) %collective-permute-start.7) | collective-permute-done | bytes 245792 | tf_op jit(solution)/shard_map/ppermute | solution.py:25
  452.5 24.5 %collective-permute-done.9 = bf16[1,1,60,2048]{3,2,0,1:T(8,128)(2,1)S(1)} collective-permute-done((bf16[1,1,60,2048]{3,2,0,1:T(8,128)(2,1)S(1)}, bf16[1,1,60,2048]{3,2,0,1:T(8,128)(2,1)S(1)}, u32[]{:S(2)}, u32[]{:S(2)}) %collective-permute-start.9) | collective-permute-done | bytes 245792 | tf_op jit(solution)/shard_map/ppermute | solution.py:25
  479.3 6.2 %collective-permute-done.11 = bf16[1,1,60,2048]{3,2,0,1:T(8,128)(2,1)S(1)} collective-permute-done((bf16[1,1,60,2048]{3,2,0,1:T(8,128)(2,1)S(1)}, bf16[1,1,60,2048]{3,2,0,1:T(8,128)(2,1)S(1)}, u32[]{:S(2)}, u32[]{:S(2)}) %collective-permute-start.11) | collective-permute-done | bytes 245792 | tf_op jit(solution)/shard_map/ppermute | solution.py:25
  493.3 9.7 %gather_fusion.1 = bf16[768,2048]{1,0:T(8,128)(2,1)} fusion(bf16[960,2048]{1,0:T(8,128)(2,1)} %reshape_reshape.3, s32[1024]{0:T(1024)S(1)} %pad_clamp_fusion), kind=kCustom, calls=%fused_computation.1.clone | custom fusion | bytes 6294528 | tf_op jit(solution)/shard_map/jit(_take)/gather | solution.py:131
  515.0 9.0 %gather_fusion = bf16[768,2048]{1,0:T(8,128)(2,1)S(1)} fusion(bf16[960,2048]{1,0:T(8,128)(2,1)} %reshape.216, s32[1024]{0:T(1024)S(1)} %pad_clamp_fusion), kind=kCustom, calls=%fused_computation.clone | custom fusion | bytes 6294528 | tf_op jit(solution)/shard_map/jit(_take)/gather | solution.py:128
  528.6 6.2 %broadcast_select_fusion.2 = (bf16[768,2048]{1,0:T(8,128)(2,1)}, f32[768,2048]{1,0:T(8,128)}) fusion(bf16[768,2048]{1,0:T(8,128)(2,1)} %gather_fusion.1, pred[768]{0:T(1024)(128)(4,1)S(1)} %get-tuple-element.131, bf16[768,2048]{1,0:T(8,128)(2,1)S(1)} %gather_fusion), kind=kLoop, calls=%fused_computation.14 | loop fusion | flops 4718592 | bytes 15729408 | tf_op jit(solution)/shard_map/jit(_take)/select_n | solution.py:131
  534.8 6.2 %reshape.235 = bf16[128,6,2048]{2,1,0:T(8,128)(2,1)} reshape(bf16[768,2048]{1,0:T(8,128)(2,1)} %get-tuple-element.151) | data formatting | bytes 6291456 | tf_op jit(solution)/shard_map/reshape | solution.py:133
  541.0 5.7 reduce_sum.69
  546.7 8.1 %reshape.236 = f32[128,6,2048]{2,1,0:T(8,128)} reshape(f32[768,2048]{1,0:T(8,128)} %get-tuple-element.152) | data formatting | bytes 12582912 | tf_op jit(solution)/shard_map/convert_element_type | solution.py:132
  554.8 7.4 %multiply_reduce_fusion = bf16[128,2048]{1,0:T(8,128)(2,1)} fusion(f32[128,6,2048]{2,1,0:T(8,128)} %reshape.236, f32[128,6]{1,0:T(8,128)S(1)} %copy.29), kind=kLoop, calls=%fused_computation.7 | loop fusion | flops 2883584 | bytes 6818816 | tf_op jit(solution)/shard_map/reduce_sum | solution.py:134
  (117 shorter events, 99.0 us)
Async XLA Ops:
  52.3 10.5 %copy-start.4 = (f32[128,6]{0,1:T(8,128)S(1)}, f32[128,6]{0,1:T(8,128)}, u32[]{:S(2)}) copy-start(f32[128,6]{0,1:T(8,128)} %param.15) | copy-start | bytes 9220
  52.3 10.7 %copy-start.3 = (bf16[128,2048]{1,0:T(8,128)(2,1)S(1)}, bf16[128,2048]{1,0:T(8,128)(2,1)}, u32[]{:S(2)}) copy-start(bf16[128,2048]{1,0:T(8,128)(2,1)} %param.13) | copy-start | bytes 1572868
  52.3 101.7 %all-to-all-start = ((bf16[16,60,2048]{2,1,0:T(8,128)(2,1)}), bf16[16,60,2048]{2,1,0:T(8,128)(2,1)}, u32[]{:S(2)}, u32[]{:S(2)}) async-start(bf16[16,60,2048]{2,1,0:T(8,128)(2,1)} %reshape.211), calls=%async_computation | async-start | bytes 8388608 | tf_op jit(solution)/shard_map/all_to_all | solution.py:89
  154.0 97.4 %all-to-all-start.2 = ((bf16[16,60,2048]{2,1,0:T(8,128)(2,1)}), bf16[16,60,2048]{2,1,0:T(8,128)(2,1)}, u32[]{:S(2)}, u32[]{:S(2)}) async-start(bf16[16,60,2048]{2,1,0:T(8,128)(2,1)} %reshape.217), calls=%async_computation.2 | async-start | bytes 8388608 | tf_op jit(solution)/shard_map/all_to_all | solution.py:90
  159.9 30.2 %all-gather.7.cloned.1.call-start = ((), (), s32[]{:S(2)}) async-start(), calls=%async_computation.7 | async-start | bytes 2359296 | tf_op jit(solution)/shard_map/all_gather | solution.py:85
  160.6 58.3 %all-gather.9.cloned.1.call-start = ((), (), s32[]{:S(2)}) async-start(), calls=%async_computation.8 | async-start | bytes 2359296 | tf_op jit(solution)/shard_map/all_gather | solution.py:86
  161.4 96.2 %all-gather.5.cloned.1.call-start = ((), (), s32[]{:S(2)}) async-start(), calls=%async_computation.6 | async-start | bytes 2359296 | tf_op jit(solution)/shard_map/all_gather | solution.py:84
  162.1 340.9 %reduce-scatter.8.cloned.1.call-start = ((), (), s32[]{:S(2)}) async-start(), calls=%async_computation.11 | async-start | bytes 4718592 | tf_op jit(solution)/shard_map/reduce_scatter | solution.py:117
  269.8 235.6 %reduce-scatter.4.cloned.1.call-start = ((), (), s32[]{:S(2)}) async-start(), calls=%async_computation.9 | async-start | bytes 4718592 | tf_op jit(solution)/shard_map/reduce_scatter | solution.py:115
  281.2 229.0 %all-to-all-start.1 = ((bf16[16,60,2048]{2,1,0:T(8,128)(2,1)}), bf16[16,60,2048]{2,1,0:T(8,128)(2,1)}, u32[]{:S(2)}, u32[]{:S(2)}) async-start(bf16[16,60,2048]{2,1,0:T(8,128)(2,1)} %convolution_convert_fusion), calls=%async_computation.1 | async-start | bytes 8388608 | tf_op jit(solution)/shard_map/all_to_all | solution.py:125
  287.1 220.7 %reduce-scatter.6.cloned.1.call-start = ((), (), s32[]{:S(2)}) async-start(), calls=%async_computation.10 | async-start | bytes 4718592 | tf_op jit(solution)/shard_map/reduce_scatter | solution.py:116
  293.2 1.4 copy-start.2
  294.6 2.3 copy-start.1
  299.3 2.0 copy-start
  302.3 58.4 %collective-permute-start = (bf16[1,1,60,2048]{3,2,0,1:T(8,128)(2,1)}, bf16[1,1,60,2048]{3,2,0,1:T(8,128)(2,1)}, u32[]{:S(2)}, u32[]{:S(2)}) collective-permute-start(bf16[1,1,60,2048]{3,2,0,1:T(8,128)(2,1)} %get-tuple-element.147), channel_id=1, source_target_pairs={{0,2},{2,4},{4,6},{6,8},{8,10},{10,12},{12,14},{14,16},{16,18},{18... | collective-permute-start | bytes 737288 | tf_op jit(solution)/shard_map/ppermute | solution.py:25
  302.4 64.0 %collective-permute-start.1 = (bf16[1,1,60,2048]{3,2,0,1:T(8,128)(2,1)}, bf16[1,1,60,2048]{3,2,0,1:T(8,128)(2,1)}, u32[]{:S(2)}, u32[]{:S(2)}) collective-permute-start(bf16[1,1,60,2048]{3,2,0,1:T(8,128)(2,1)} %get-tuple-element.146), channel_id=1, source_target_pairs={{0,4},{2,6},{4,8},{6,10},{8,12},{10,14},{12,16},{14,18},{16,20},{1... | collective-permute-start | bytes 737288 | tf_op jit(solution)/shard_map/ppermute | solution.py:25
  304.1 183.5 %collective-permute-start.14 = (bf16[1,1,60,2048]{3,2,0,1:T(8,128)(2,1)S(1)}, bf16[1,1,60,2048]{3,2,0,1:T(8,128)(2,1)S(1)}, u32[]{:S(2)}, u32[]{:S(2)}) collective-permute-start(bf16[1,1,60,2048]{3,2,0,1:T(8,128)(2,1)S(1)} %get-tuple-element.133), channel_id=1, source_target_pairs={{0,30},{2,0},{4,2},{6,4},{8,6},{10,8},{12,10},{14,12},{16,14},{18,... | collective-permute-start | bytes 737288 | tf_op jit(solution)/shard_map/ppermute | solution.py:25
  304.1 182.8 %collective-permute-start.13 = (bf16[1,1,60,2048]{3,2,0,1:T(8,128)(2,1)S(1)}, bf16[1,1,60,2048]{3,2,0,1:T(8,128)(2,1)S(1)}, u32[]{:S(2)}, u32[]{:S(2)}) collective-permute-start(bf16[1,1,60,2048]{3,2,0,1:T(8,128)(2,1)S(1)} %get-tuple-element.134), channel_id=1, source_target_pairs={{0,28},{2,30},{4,0},{6,2},{8,4},{10,6},{12,8},{14,10},{16,12},{18,... | collective-permute-start | bytes 737288 | tf_op jit(solution)/shard_map/ppermute | solution.py:25
  304.7 181.5 %collective-permute-start.12 = (bf16[1,1,60,2048]{3,2,0,1:T(8,128)(2,1)S(1)}, bf16[1,1,60,2048]{3,2,0,1:T(8,128)(2,1)S(1)}, u32[]{:S(2)}, u32[]{:S(2)}) collective-permute-start(bf16[1,1,60,2048]{3,2,0,1:T(8,128)(2,1)S(1)} %get-tuple-element.135), channel_id=1, source_target_pairs={{0,26},{2,28},{4,30},{6,0},{8,2},{10,4},{12,6},{14,8},{16,10},{18,... | collective-permute-start | bytes 737288 | tf_op jit(solution)/shard_map/ppermute | solution.py:25
  360.8 11.1 %collective-permute-start.2 = (bf16[1,1,60,2048]{3,2,0,1:T(8,128)(2,1)S(1)}, bf16[1,1,60,2048]{3,2,0,1:T(8,128)(2,1)S(1)}, u32[]{:S(2)}, u32[]{:S(2)}) collective-permute-start(bf16[1,1,60,2048]{3,2,0,1:T(8,128)(2,1)S(1)} %get-tuple-element.145), channel_id=1, source_target_pairs={{0,6},{2,8},{4,10},{6,12},{8,14},{10,16},{12,18},{14,20},{16,22},{... | collective-permute-start | bytes 737288 | tf_op jit(solution)/shard_map/ppermute | solution.py:25
  366.4 31.5 %collective-permute-start.3 = (bf16[1,1,60,2048]{3,2,0,1:T(8,128)(2,1)S(1)}, bf16[1,1,60,2048]{3,2,0,1:T(8,128)(2,1)S(1)}, u32[]{:S(2)}, u32[]{:S(2)}) collective-permute-start(bf16[1,1,60,2048]{3,2,0,1:T(8,128)(2,1)S(1)} %get-tuple-element.144), channel_id=1, source_target_pairs={{0,8},{2,10},{4,12},{6,14},{8,16},{10,18},{12,20},{14,22},{16,24},... | collective-permute-start | bytes 737288 | tf_op jit(solution)/shard_map/ppermute | solution.py:25
  371.9 31.8 %collective-permute-start.4 = (bf16[1,1,60,2048]{3,2,0,1:T(8,128)(2,1)S(1)}, bf16[1,1,60,2048]{3,2,0,1:T(8,128)(2,1)S(1)}, u32[]{:S(2)}, u32[]{:S(2)}) collective-permute-start(bf16[1,1,60,2048]{3,2,0,1:T(8,128)(2,1)S(1)} %get-tuple-element.143), channel_id=1, source_target_pairs={{0,10},{2,12},{4,14},{6,16},{8,18},{10,20},{12,22},{14,24},{16,26}... | collective-permute-start | bytes 737288 | tf_op jit(solution)/shard_map/ppermute | solution.py:25
  397.8 20.8 %collective-permute-start.5 = (bf16[1,1,60,2048]{3,2,0,1:T(8,128)(2,1)S(1)}, bf16[1,1,60,2048]{3,2,0,1:T(8,128)(2,1)S(1)}, u32[]{:S(2)}, u32[]{:S(2)}) collective-permute-start(bf16[1,1,60,2048]{3,2,0,1:T(8,128)(2,1)S(1)} %get-tuple-element.142), channel_id=1, source_target_pairs={{0,12},{2,14},{4,16},{6,18},{8,20},{10,22},{12,24},{14,26},{16,28}... | collective-permute-start | bytes 737288 | tf_op jit(solution)/shard_map/ppermute | solution.py:25
  403.7 25.1 %collective-permute-start.6 = (bf16[1,1,60,2048]{3,2,0,1:T(8,128)(2,1)S(1)}, bf16[1,1,60,2048]{3,2,0,1:T(8,128)(2,1)S(1)}, u32[]{:S(2)}, u32[]{:S(2)}) collective-permute-start(bf16[1,1,60,2048]{3,2,0,1:T(8,128)(2,1)S(1)} %get-tuple-element.141), channel_id=1, source_target_pairs={{0,14},{2,16},{4,18},{6,20},{8,22},{10,24},{12,26},{14,28},{16,30}... | collective-permute-start | bytes 737288 | tf_op jit(solution)/shard_map/ppermute | solution.py:25
  418.7 32.3 %collective-permute-start.7 = (bf16[1,1,60,2048]{3,2,0,1:T(8,128)(2,1)S(1)}, bf16[1,1,60,2048]{3,2,0,1:T(8,128)(2,1)S(1)}, u32[]{:S(2)}, u32[]{:S(2)}) collective-permute-start(bf16[1,1,60,2048]{3,2,0,1:T(8,128)(2,1)S(1)} %get-tuple-element.140), channel_id=1, source_target_pairs={{0,16},{2,18},{4,20},{6,22},{8,24},{10,26},{12,28},{14,30},{16,0},... | collective-permute-start | bytes 737288 | tf_op jit(solution)/shard_map/ppermute | solution.py:25
  428.8 22.9 %collective-permute-start.8 = (bf16[1,1,60,2048]{3,2,0,1:T(8,128)(2,1)S(1)}, bf16[1,1,60,2048]{3,2,0,1:T(8,128)(2,1)S(1)}, u32[]{:S(2)}, u32[]{:S(2)}) collective-permute-start(bf16[1,1,60,2048]{3,2,0,1:T(8,128)(2,1)S(1)} %get-tuple-element.139), channel_id=1, source_target_pairs={{0,18},{2,20},{4,22},{6,24},{8,26},{10,28},{12,30},{14,0},{16,2},{... | collective-permute-start | bytes 737288 | tf_op jit(solution)/shard_map/ppermute | solution.py:25
  451.0 26.0 %collective-permute-start.9 = (bf16[1,1,60,2048]{3,2,0,1:T(8,128)(2,1)S(1)}, bf16[1,1,60,2048]{3,2,0,1:T(8,128)(2,1)S(1)}, u32[]{:S(2)}, u32[]{:S(2)}) collective-permute-start(bf16[1,1,60,2048]{3,2,0,1:T(8,128)(2,1)S(1)} %get-tuple-element.138), channel_id=1, source_target_pairs={{0,20},{2,22},{4,24},{6,26},{8,28},{10,30},{12,0},{14,2},{16,4},{1... | collective-permute-start | bytes 737288 | tf_op jit(solution)/shard_map/ppermute | solution.py:25
  451.8 26.8 %collective-permute-start.10 = (bf16[1,1,60,2048]{3,2,0,1:T(8,128)(2,1)S(1)}, bf16[1,1,60,2048]{3,2,0,1:T(8,128)(2,1)S(1)}, u32[]{:S(2)}, u32[]{:S(2)}) collective-permute-start(bf16[1,1,60,2048]{3,2,0,1:T(8,128)(2,1)S(1)} %get-tuple-element.137), channel_id=1, source_target_pairs={{0,22},{2,24},{4,26},{6,28},{8,30},{10,0},{12,2},{14,4},{16,6},{18... | collective-permute-start | bytes 737288 | tf_op jit(solution)/shard_map/ppermute | solution.py:25
  477.0 8.5 %collective-permute-start.11 = (bf16[1,1,60,2048]{3,2,0,1:T(8,128)(2,1)S(1)}, bf16[1,1,60,2048]{3,2,0,1:T(8,128)(2,1)S(1)}, u32[]{:S(2)}, u32[]{:S(2)}) collective-permute-start(bf16[1,1,60,2048]{3,2,0,1:T(8,128)(2,1)S(1)} %get-tuple-element.136), channel_id=1, source_target_pairs={{0,24},{2,26},{4,28},{6,30},{8,0},{10,2},{12,4},{14,6},{16,8},{18,... | collective-permute-start | bytes 737288 | tf_op jit(solution)/shard_map/ppermute | solution.py:25
Sparse Core Ops, SparseCore 0:
  162.3 27.8 all-gather.6
  191.7 27.2 all-gather.8
  220.5 27.1 all-gather.4
  269.9 43.7 reduce-scatter.7
  315.9 43.3 reduce-scatter.3
  361.4 43.3 reduce-scatter.5
